TPU v7x, 32 devices: a whole 2x2x4 slice. The times are simulated.
32 devices in a mesh: grp: 2 (over y), gx: 16 (over z, x, core).
Axes of the slice: x: 2, y: 2, z: 4, core: 2. Of those that a mesh axis runs over, the one named last changes fastest.
Arguments:
- volume: float32 [512, 896], P(('grp', 'gx')), parts along dimension 0, may hold values from -45 to 45
- bank: float32 [8, 4096], P(None, 'gx'), may hold values from -43 to 43
- orient: int32 [8], replicated, may hold values from 0 to 47
- bank_id: int32 [8], replicated, may hold values from 0 to 7, each once
- counts: int32 [8], replicated, may hold values from 1 to 16
Outputs:
- fields: float32 [4, 512, 896], P(None, ('grp', 'gx')), parts along dimension 1
There are 2 independent parts, one for each index of `grp`. A program takes and returns all parts, laid end to end along the dimension named above; an argument that names none is the same for every part. Nothing has to cross between parts.
Inputs may be any that keep to these rules, and one draw needn't show every extreme that they name: `bank_id`: each of the 8 base templates is named by exactly one list entry.
All inputs are finite; a program needn't handle non-finite values.
Results may differ from a plain program's by a relative error of at most 0.0003.
Values sent between devices are 32-bit elements; how exact they have to be, the bound alone decides.
No kernel may reach another device: no remote copies, remote signals or barrier semaphores. Data moves between devices by JAX's collectives and lax.ppermute only.
A program may use at most 64 MiB of HBM per device.

v0:
```python
import math
import jax
import jax.numpy as jnp
import numpy as np
from jax import lax
from jax.sharding import PartitionSpec as P

BY = 8
BZ = 112
TS = 16
NT = 8
FIELDS = 4
epsilon = 1e-05
sharpness = 80.0
AXIS_ORDERS = np.array([[0, 1, 2], [0, 2, 1], [1, 0, 2], [1, 2, 0], [2, 0, 1], [2, 1, 0]], np.int32)


def extended(x, sides, width):
    for axis, dim in sides:
        size, length = (lax.axis_size(axis), x.shape[dim])
        up = [(i, (i + 1) % size) for i in range(size - 1)]
        down = [(j, i) for i, j in up]
        last = lax.slice_in_dim(x, length - width, length, axis=dim)
        leading = lax.slice_in_dim(x, 0, width, axis=dim)
        before = lax.ppermute(last, axis, up)
        after = lax.ppermute(leading, axis, down)
        x = jnp.concatenate([before, x, after], axis=dim)
    return x


def padded_length(length):
    return -(-length // 128) * 128


def rotate_template(flat_base, orient_one):
    coords = jnp.arange(TS**3, dtype=jnp.int32)
    index_set = jnp.stack([coords // (TS * TS), coords // TS % TS, coords % TS])
    order_row = orient_one // 8
    flip_set = orient_one % 8
    picked = (jnp.arange(6, dtype=jnp.int32) == order_row).astype(jnp.int32)
    ordering = jnp.sum(picked[:, None] * jnp.asarray(AXIS_ORDERS), axis=0)
    source = jnp.zeros_like(coords)
    for axis_num in range(3):
        select = (ordering[axis_num] == jnp.arange(3, dtype=jnp.int32)).astype(jnp.int32)
        chosen = jnp.sum(select[:, None] * index_set, axis=0)
        flipped = flip_set // 2**axis_num % 2
        placed = chosen + flipped * (TS - 1 - 2 * chosen)
        source = source * TS + placed
    return flat_base[source]


def normalized_kernel(flat_base, orient_one):
    rotated = rotate_template(flat_base, orient_one)
    centered = rotated - jnp.mean(rotated)
    return centered / jnp.sqrt(jnp.sum(centered * centered) + epsilon)


def wave_tables(positions, targets, period, direction):
    turns = (positions[:, None] * targets[None, :] % period).astype(jnp.float32)
    phase = 2.0 * math.pi / period * turns
    return (jnp.cos(phase), direction * jnp.sin(phase))


def band_table(positions, targets, period):
    offset = (positions[:, None] - targets[None, :]) % period
    return (offset < TS).astype(jnp.float32)


def contract(letters, data, table):
    return jnp.einsum(letters, data, table, precision=lax.Precision.HIGHEST)


def spectrum_along(real_part, imag_part, cos_table, sin_table, letters):
    new_real = contract(letters, real_part, cos_table) - contract(letters, imag_part, sin_table)
    new_imag = contract(letters, real_part, sin_table) + contract(letters, imag_part, cos_table)
    return (new_real, new_imag)


def local(volume, bank, orient, bank_id, counts):
    rows_x = volume.shape[0]
    half = TS // 2
    grid = volume.reshape(rows_x, BY, BZ)
    len_x = rows_x + TS
    len_y = BY + TS
    len_z = padded_length(BZ + TS)
    gathered = lax.all_gather(bank, "gx", axis=1, tiled=True)
    kernels = jax.vmap(normalized_kernel)(gathered[bank_id], orient)
    field_in = extended(grid, (("gx", 0),), half)
    pos_x = jnp.arange(len_x, dtype=jnp.int32)
    out_x = jnp.arange(rows_x, dtype=jnp.int32)
    pos_y = half + jnp.arange(BY, dtype=jnp.int32)
    pos_z = half + jnp.arange(BZ, dtype=jnp.int32)
    freq_x = jnp.arange(len_x, dtype=jnp.int32)
    freq_y = jnp.arange(len_y, dtype=jnp.int32)
    freq_z = jnp.arange(len_z, dtype=jnp.int32)
    tmpl_pos = jnp.arange(TS, dtype=jnp.int32)
    cos_z, sin_z = wave_tables(pos_z, freq_z, len_z, -1.0)
    cos_y, sin_y = wave_tables(pos_y, freq_y, len_y, -1.0)
    cos_x, sin_x = wave_tables(pos_x, freq_x, len_x, -1.0)
    vol_re = contract("xyz,zk->xyk", field_in, cos_z)
    vol_im = contract("xyz,zk->xyk", field_in, sin_z)
    vol_re, vol_im = spectrum_along(vol_re, vol_im, cos_y, sin_y, "xyk,yj->xjk")
    vol_re, vol_im = spectrum_along(vol_re, vol_im, cos_x, sin_x, "xjk,xi->ijk")
    kcos_z, ksin_z = wave_tables(tmpl_pos, freq_z, len_z, -1.0)
    kcos_y, ksin_y = wave_tables(tmpl_pos, freq_y, len_y, -1.0)
    kcos_x, ksin_x = wave_tables(tmpl_pos, freq_x, len_x, -1.0)
    icos_y, isin_y = wave_tables(freq_y, jnp.arange(BY, dtype=jnp.int32), len_y, 1.0)
    icos_x, isin_x = wave_tables(freq_x, out_x, len_x, 1.0)
    icos_z, isin_z = wave_tables(freq_z, jnp.arange(BZ, dtype=jnp.int32), len_z, 1.0)
    inverse_scale = 1.0 / (len_x * len_y * len_z)

    def correlate(kernel_flat):
        kernel = kernel_flat.reshape(TS, TS, TS)
        kernel_re = contract("xyz,zk->xyk", kernel, kcos_z)
        kernel_im = contract("xyz,zk->xyk", kernel, ksin_z)
        kernel_re, kernel_im = spectrum_along(kernel_re, kernel_im, kcos_y, ksin_y, "xyk,yj->xjk")
        kernel_re, kernel_im = spectrum_along(kernel_re, kernel_im, kcos_x, ksin_x, "xjk,xi->ijk")
        prod_re = kernel_re * vol_re + kernel_im * vol_im
        prod_im = kernel_re * vol_im - kernel_im * vol_re
        prod_re, prod_im = spectrum_along(prod_re, prod_im, icos_y, isin_y, "ijk,jn->ink")
        prod_re, prod_im = spectrum_along(prod_re, prod_im, icos_x, isin_x, "ink,im->mnk")
        real_out = contract("mnk,kz->mnz", prod_re, icos_z) - contract(
            "mnk,kz->mnz", prod_im, isin_z
        )
        return real_out * inverse_scale

    numer = lax.map(correlate, kernels)
    squares = field_in * field_in
    energy = contract(
        "xyz,zn->xyn", squares, band_table(pos_z, jnp.arange(BZ, dtype=jnp.int32), len_z)
    )
    energy = contract(
        "xyn,ym->xmn", energy, band_table(pos_y, jnp.arange(BY, dtype=jnp.int32), len_y)
    )
    energy = contract("xmn,xl->lmn", energy, band_table(pos_x, out_x, len_x))
    scores = numer / jnp.sqrt(energy + epsilon)[None]
    weights = counts.astype(jnp.float32)
    weighted = weights[:, None, None, None] * jnp.exp(sharpness * scores)
    grouped = jnp.sum(weighted.reshape(FIELDS, NT // FIELDS, rows_x, BY, BZ), axis=1)
    totals = jnp.sum(weights.reshape(FIELDS, NT // FIELDS), axis=1)
    fields = jnp.log(grouped / totals[:, None, None, None])
    return fields.reshape(FIELDS, rows_x, BY * BZ)


def solution(mesh):
    in_specs = (P(("grp", "gx"), None), P(None, "gx"), P(), P(), P())
    out_specs = P(None, ("grp", "gx"), None)
    return jax.shard_map(local, mesh=mesh, in_specs=in_specs, out_specs=out_specs, check_vma=False)
```

profile of v0, /device:TPU:0, one launch (start us, length us, event | category | flops | bytes accessed | tf_op | source)
XLA Modules:
  0.0 316.0 jit_solution(17705312637097414959)
XLA Ops:
  0.0 0.8 fusion.433
  0.8 2.3 collective-permute-start
  3.3 1.3 collective-permute-start.1
  4.6 0.7 compare_select_fusion.3
  5.3 0.7 and_select_fusion.8
  6.1 0.8 multiply_reduce_fusion.4
  6.9 25.6 %all_gather.3 = f32[8,4096]{1,0:T(8,128)S(1)} all-gather(f32[8,256]{1,0:T(8,128)} %param.9), channel_id=1, replica_groups=mesh['grp'=2,'gx'=16] {'gx'}, dimensions={1}, use_global_device_ids=true | all-gather | bytes 139264 | tf_op jit(solution)/shard_map/all_gather | solution.py:86
  32.9 0.6 gather_fusion
  33.5 200.1 %gather_fusion.1 = f32[32768]{0:T(1024)S(1)} fusion(f32[8,4096]{1,0:T(8,128)S(1)} %gather_fusion, s32[32768]{0:T(1024)S(1)} %bitcast.250), kind=kCustom, calls=%fused_computation.1 | custom fusion | bytes 524288 | tf_op jit(solution)/shard_map/vmap()/gather | solution.py:49
  235.9 0.6 fusion.332
  236.6 0.6 fusion.336
  237.2 0.6 fusion.250
  239.8 0.6 fusion.249
  240.5 0.6 convolution_subtract_fusion.5
  241.6 73.3 %while.12 = (s32[]{:T(128)}, f32[8,16,8,112]{3,2,1,0:T(8,128)S(1)}, f32[8,4096]{1,0:T(8,128)S(1)}, f32[32,24,128]{2,0,1:T(8,128)S(1)}, f32[32,24,128]{2,0,1:T(8,128)S(1)}, /*index=5*/s32[]{:T(128)}) while((s32[]{:T(128)}, f32[8,16,8,112]{3,2,1,0:T(8,128)S(1)}, f32[8,4096]{1,0:T(8,128)S(1)}, ...), condition=%wide.region_7.8_spmd.clone.clone, body=%wide.region_6.7_spmd.clone.clone.sunk | while | flops 234336256 | bytes 10379349 | solution.py:127
  246.0 0.7 multiply_subtract_fusion.2
  255.1 0.7 multiply_subtract_fusion.2
  264.3 0.7 multiply_subtract_fusion.2
  273.4 0.7 multiply_subtract_fusion.2
  282.5 0.7 multiply_subtract_fusion.2
  291.7 0.7 multiply_subtract_fusion.2
  300.8 0.7 multiply_subtract_fusion.2
  310.0 0.7 multiply_subtract_fusion.2
  315.2 0.8 divide_log_fusion
  (216 shorter events, 71.7 us)
Async XLA Ops:
  0.8 233.9 %collective-permute-start = (f32[8,8,112]{2,1,0:T(8,128)S(1)}, f32[8,8,112]{2,1,0:T(8,128)S(1)}, u32[]{:S(2)}, u32[]{:S(2)}) collective-permute-start(f32[8,8,112]{2,1,0:T(8,128)S(1)} %slice.34), channel_id=1, source_target_pairs={{0,1},{1,2},{2,3},{3,4},{4,5},{5,6},{6,7},{7,8},{8,9},{9,10},{10,1... | collective-permute-start | bytes 86024 | tf_op jit(solution)/shard_map/ppermute | solution.py:25
  3.3 231.5 %collective-permute-start.1 = (f32[8,8,112]{2,1,0:T(8,128)S(1)}, f32[8,8,112]{2,1,0:T(8,128)S(1)}, u32[]{:S(2)}, u32[]{:S(2)}) collective-permute-start(f32[8,8,112]{2,1,0:T(8,128)S(1)} %slice.36), channel_id=1, source_target_pairs={{1,0},{2,1},{3,2},{4,3},{5,4},{6,5},{7,6},{8,7},{9,8},{10,9},{11,1... | collective-permute-start | bytes 86024 | tf_op jit(solution)/shard_map/ppermute | solution.py:26
  233.6 0.8 copy-start
  233.6 0.9 copy-start.1
where the time goes:
time: 316 us
  local copies, waits for them, and re-layouts  203 us (64%)
  matrix products  77.2 us (24%)
  blocking collectives  25.6 us (8%)
  other arithmetic  4.22 us (1%)
  starting transfers between devices  3.63 us (1%)
    gather x2, local copies, waits for them, and re-layouts, rotate_template(): return flat_base[source]  200 us
    dot_general x173, matrix products, contract(): return jnp.einsum(letters, data, table, precision=lax.Precision.HIGHEST)  77.2 us
    all_gather x1, blocking collectives, local(): gathered = lax.all_gather(bank, 'gx', axis=1, tiled=True)  25.6 us
  transfers between devices with their start and end apart: 2, of which 0 were waited for; matrix products, arithmetic and copies ran while one was open for 65% of the time, Pallas kernels for 0%

commit v1 on v0

--- a/solution.py
+++ b/solution.py
@@ -83,7 +83,15 @@
     len_x = rows_x + TS
     len_y = BY + TS
     len_z = padded_length(BZ + TS)
-    gathered = lax.all_gather(bank, "gx", axis=1, tiled=True)
+    ways, here = (lax.axis_size("gx"), lax.axis_index("gx"))
+    grown, reach = (bank, 1)
+    while reach < ways:
+        theirs = lax.ppermute(grown, "gx", [(d, d ^ reach) for d in range(ways)])
+        mine_first = jnp.concatenate([grown, theirs], axis=1)
+        theirs_first = jnp.concatenate([theirs, grown], axis=1)
+        grown = jnp.where(here & reach == 0, mine_first, theirs_first)
+        reach = 2 * reach
+    gathered = grown
     kernels = jax.vmap(normalized_kernel)(gathered[bank_id], orient)
     field_in = extended(grid, (("gx", 0),), half)
     pos_x = jnp.arange(len_x, dtype=jnp.int32)

time: 316 us -> 305 us (0.965)
  blocking collectives: 25.6 us -> 0 us
  starting transfers between devices: 3.63 us -> 14.2 us
  waiting for transfers between devices: 0.01 us -> 3.95 us
    all_gather x1 -> x0, blocking collectives: 25.6 us -> none  [local(): gathered = lax.all_gather(bank, 'gx', axis=1, tiled=True)]
    ppermute x0 -> x4, starting transfers between devices: none -> 10.9 us  [local(): theirs = lax.ppermute(grown, 'gx', [(d, d ^ reach) for d in range(ways)])]
    ppermute x0 -> x4, waiting for transfers between devices: none -> 3.95 us  [local(): theirs = lax.ppermute(grown, 'gx', [(d, d ^ reach) for d in range(ways)])]
  transfers between devices with their start and end apart: 2 -> 6, of which waited for: 0 -> 2; matrix products, arithmetic and copies ran while one was open for 65% -> 3% of each run, Pallas kernels for 0% -> 0%
where the time goes in v1:
time: 305 us
  local copies, waits for them, and re-layouts  204 us (67%)
  matrix products  77.2 us (25%)
  starting transfers between devices  14.2 us (5%)
  other arithmetic  4.26 us (1%)
  waiting for transfers between devices  3.95 us (1%)
    gather x2, local copies, waits for them, and re-layouts, rotate_template(): return flat_base[source]  200 us
    dot_general x173, matrix products, contract(): return jnp.einsum(letters, data, table, precision=lax.Precision.HIGHEST)  77.2 us
    ppermute x4, starting transfers between devices, local(): theirs = lax.ppermute(grown, 'gx', [(d, d ^ reach) for d in range(ways)])  10.9 us
  transfers between devices with their start and end apart: 6, of which 2 were waited for; matrix products, arithmetic and copies ran while one was open for 3% of the time, Pallas kernels for 0%

profile of v1, /device:TPU:0, one launch (start us, length us, event | category | flops | bytes accessed | tf_op | source)
XLA Modules:
  0.0 305.0 jit_solution(11126233292213459844)
XLA Ops:
  0.5 0.8 fusion.433
  1.3 2.0 collective-permute-start.4
  3.3 1.3 collective-permute-start.5
  4.7 0.7 compare_select_fusion.3
  5.3 0.7 and_select_fusion.8
  6.1 0.8 multiply_reduce_fusion.4
  7.7 4.8 %collective-permute-start.1 = (f32[8,512]{1,0:T(8,128)S(1)}, f32[8,512]{1,0:T(8,128)S(1)}, u32[]{:S(2)}, u32[]{:S(2)}) collective-permute-start(f32[8,512]{1,0:T(8,128)S(1)} %maximum_select_fusion.3), channel_id=1, source_target_pairs={{0,2},{1,3},{2,0},{3,1},{4,6},{5,7},{6,4},{7,5},{8,10},{9,11},{10,... | collective-permute-start | bytes 49160 | tf_op jit(solution)/shard_map/ppermute | solution.py:89
  12.9 1.3 collective-permute-done.1
  14.3 3.0 collective-permute-start.2
  18.4 0.6 fusion.332
  19.7 0.6 fusion.250
  23.9 2.7 collective-permute-start.3
  26.8 2.6 collective-permute-done.3
  30.0 200.3 %gather_fusion.1 = f32[32768]{0:T(1024)S(1)} fusion(f32[8,4096]{1,0:T(8,128)S(1)} %gather_fusion, s32[32768]{0:T(1024)S(1)} %bitcast.250), kind=kCustom, calls=%fused_computation.1 | custom fusion | bytes 524288 | tf_op jit(solution)/shard_map/vmap()/gather | solution.py:49
  230.8 73.1 %while.12 = (s32[]{:T(128)}, f32[8,16,8,112]{3,2,1,0:T(8,128)S(1)}, f32[8,4096]{1,0:T(8,128)S(1)}, f32[32,24,128]{2,0,1:T(8,128)S(1)}, f32[32,24,128]{2,0,1:T(8,128)S(1)}, /*index=5*/s32[]{:T(128)}) while((s32[]{:T(128)}, f32[8,16,8,112]{3,2,1,0:T(8,128)S(1)}, f32[8,4096]{1,0:T(8,128)S(1)}, ...), condition=%wide.region_7.8_spmd.clone.clone, body=%wide.region_6.7_spmd.clone.clone.sunk | while | flops 234336256 | bytes 10379349 | solution.py:135
  235.0 0.7 multiply_subtract_fusion.2
  244.2 0.7 multiply_subtract_fusion.2
  253.3 0.7 multiply_subtract_fusion.2
  262.4 0.7 multiply_subtract_fusion.2
  271.6 0.7 multiply_subtract_fusion.2
  280.7 0.7 multiply_subtract_fusion.2
  289.8 0.7 multiply_subtract_fusion.2
  299.0 0.7 multiply_subtract_fusion.2
  304.2 0.8 divide_log_fusion
  (229 shorter events, 74.7 us)
Async XLA Ops:
  0.0 7.4 %collective-permute-start = (f32[8,256]{1,0:T(8,128)}, f32[8,256]{1,0:T(8,128)S(1)}, u32[]{:S(2)}, u32[]{:S(2)}) collective-permute-start(f32[8,256]{1,0:T(8,128)} %param.9), channel_id=1, source_target_pairs={{0,1},{1,0},{2,3},{3,2},{4,5},{5,4},{6,7},{7,6},{8,9},{9,8},{10,11... | collective-permute-start | bytes 24584 | tf_op jit(solution)/shard_map/ppermute | solution.py:89
  1.3 16.0 %collective-permute-start.4 = (f32[8,8,112]{2,1,0:T(8,128)S(1)}, f32[8,8,112]{2,1,0:T(8,128)S(1)}, u32[]{:S(2)}, u32[]{:S(2)}) collective-permute-start(f32[8,8,112]{2,1,0:T(8,128)S(1)} %slice.34), channel_id=1, source_target_pairs={{0,1},{1,2},{2,3},{3,4},{4,5},{5,6},{6,7},{7,8},{8,9},{9,10},{10,1... | collective-permute-start | bytes 86024 | tf_op jit(solution)/shard_map/ppermute | solution.py:25
  3.3 14.0 %collective-permute-start.5 = (f32[8,8,112]{2,1,0:T(8,128)S(1)}, f32[8,8,112]{2,1,0:T(8,128)S(1)}, u32[]{:S(2)}, u32[]{:S(2)}) collective-permute-start(f32[8,8,112]{2,1,0:T(8,128)S(1)} %slice.36), channel_id=1, source_target_pairs={{1,0},{2,1},{3,2},{4,3},{5,4},{6,5},{7,6},{8,7},{9,8},{10,9},{11,1... | collective-permute-start | bytes 86024 | tf_op jit(solution)/shard_map/ppermute | solution.py:26
  7.0 0.7 copy-start.1
  7.0 5.5 %copy-start = (f32[16,896]{1,0:T(8,128)S(1)}, f32[16,896]{1,0:T(8,128)}, u32[]{:S(2)}) copy-start(f32[16,896]{1,0:T(8,128)} %param.8) | copy-start | bytes 172036
  7.1 5.6 %copy-start.2 = (s32[8]{0:T(128)S(1)}, s32[8]{0:T(128)}, u32[]{:S(2)}) copy-start(s32[8]{0:T(128)} %param.12) | copy-start | bytes 100
  7.7 6.5 %collective-permute-start.1 = (f32[8,512]{1,0:T(8,128)S(1)}, f32[8,512]{1,0:T(8,128)S(1)}, u32[]{:S(2)}, u32[]{:S(2)}) collective-permute-start(f32[8,512]{1,0:T(8,128)S(1)} %maximum_select_fusion.3), channel_id=1, source_target_pairs={{0,2},{1,3},{2,0},{3,1},{4,6},{5,7},{6,4},{7,5},{8,10},{9,11},{10,... | collective-permute-start | bytes 49160 | tf_op jit(solution)/shard_map/ppermute | solution.py:89
  14.3 9.6 %collective-permute-start.2 = (f32[8,1024]{1,0:T(8,128)S(1)}, f32[8,1024]{1,0:T(8,128)S(1)}, u32[]{:S(2)}, u32[]{:S(2)}) collective-permute-start(f32[8,1024]{1,0:T(8,128)S(1)} %maximum_select_fusion.2), channel_id=1, source_target_pairs={{0,4},{1,5},{2,6},{3,7},{4,0},{5,1},{6,2},{7,3},{8,12},{9,13},{10,... | collective-permute-start | bytes 98312 | tf_op jit(solution)/shard_map/ppermute | solution.py:89
  23.9 5.5 %collective-permute-start.3 = (f32[8,2048]{1,0:T(8,128)S(1)}, f32[8,2048]{1,0:T(8,128)S(1)}, u32[]{:S(2)}, u32[]{:S(2)}) collective-permute-start(f32[8,2048]{1,0:T(8,128)S(1)} %maximum_select_fusion.1), channel_id=1, source_target_pairs={{0,8},{1,9},{2,10},{3,11},{4,12},{5,13},{6,14},{7,15},{8,0},{9,1},... | collective-permute-start | bytes 196616 | tf_op jit(solution)/shard_map/ppermute | solution.py:89
